TPU v7x, 512 devices: a whole 4x8x8 slice. The times are simulated.
512 devices in a mesh: req: 64 (over x, y, core), tp: 8 (over z).
Axes of the slice: x: 4, y: 8, z: 8, core: 2. Of those that a mesh axis runs over, the one named last changes fastest.
Arguments:
- vit_context: bfloat16 [32768, 4096], P('req', 'tp'), may hold values from -6 to 6
- vision_residual: bfloat16 [32768, 4096], P('req', 'tp'), may hold values from -75 to 75
- out_weight: bfloat16 [4096, 4096], P('tp', 'req'), may hold values from -0.09375 to 0.09375
- layer_scale: float32 [4096], P('tp'), may hold values from 0.2 to 2
- prompt: bfloat16 [64, 256, 4096], P('req', None, 'tp'), may hold values from -75 to 75
- prompt_len: int32 [64], P('req'), may hold values from 128 to 256
- image_at: int32 [64], P('req'), may hold values from 0 to 128
- grid_sizes: int32 [128, 2], replicated, may hold values from 7 to 8, as said below
- image_owner: int32 [128], replicated, may hold values from 0 to 63, as said below
- norm_gain: float32 [4096], replicated, may hold values from 0.5 to 1.5
- qkv_weight: bfloat16 [4096, 6144], P('req', 'tp'), may hold values from -0.09375 to 0.09375
Outputs:
- qkv: bfloat16 [24576, 6144], P('req', 'tp')
Inputs may be any that keep to these rules, and one draw needn't show every extreme that they name: `image_owner`: each request owns exactly 2 images. `grid_sizes`: each side is 7 or 8; in every draw the images of some request are all 8 by 8, so that request has exactly 128 merged rows.
All inputs are finite; a program needn't handle non-finite values.
Results may differ from a plain program's by a relative error of at most 0.008.
Values may be sent and summed in bfloat16 or wider, within the bound.
No kernel may reach another device: no remote copies, remote signals or barrier semaphores. Data moves between devices by JAX's collectives and lax.ppermute only.
A program may use at most 64 MiB of HBM per device.

v0:
```python
import jax
import jax.numpy as jnp
from jax import lax
from jax.sharding import PartitionSpec as P

HEAD = 128
GROUP = 4
IMG_MAX = 128


def request_plan(grid_sizes, image_owner, requests):
    image_rows = grid_sizes[:, 0] * grid_sizes[:, 1]
    member = (image_owner[:, None] == jnp.arange(requests, dtype=jnp.int32)[None, :]).astype(
        jnp.int32
    )
    counts = jnp.sum(image_rows[:, None] * member, axis=0)
    starts = jnp.cumsum(counts) - counts
    return (counts, starts)


def rope_tables(count):
    half_size = HEAD // 2
    exponent = jnp.arange(half_size, dtype=jnp.float32) * (2.0 / HEAD)
    frequency = jnp.exp(-exponent * jnp.log(jnp.float32(500000.0)))
    angles = jnp.arange(count, dtype=jnp.float32)[:, None] * frequency[None, :]
    return (jnp.cos(angles), jnp.sin(angles))


def apply_rope(projected, cosine_table, sine_table):
    seq_rows = projected.shape[0]
    head_blocks = projected.reshape(seq_rows, -1, GROUP + 2, HEAD)
    turning = head_blocks[:, :, : GROUP + 1, :]
    first_half = turning[..., : HEAD // 2]
    second_half = turning[..., HEAD // 2 :]
    cosine_wide = cosine_table[:, None, None, :]
    sine_wide = sine_table[:, None, None, :]
    turned = jnp.concatenate(
        [
            first_half * cosine_wide - second_half * sine_wide,
            second_half * cosine_wide + first_half * sine_wide,
        ],
        axis=-1,
    )
    head_blocks = jnp.concatenate([turned, head_blocks[:, :, GROUP + 1 :, :]], axis=2)
    return head_blocks.reshape(seq_rows, -1)


def normalize(embedded, norm_gain):
    values = embedded.astype(jnp.float32)
    mean_square = jnp.mean(values * values, axis=-1, keepdims=True)
    return (values * lax.rsqrt(mean_square + 1e-05) * norm_gain[None, :]).astype(jnp.bfloat16)


def shards(
    vit_context,
    vision_residual,
    out_weight,
    layer_scale,
    prompt,
    prompt_len,
    image_at,
    grid_sizes,
    image_owner,
    norm_gain,
    qkv_weight,
):
    requests = lax.axis_size("req")
    device_index = lax.axis_index("req")
    feature_width = vit_context.shape[1]
    merged_context = jnp.mean(
        vit_context.astype(jnp.float32).reshape(-1, 4, feature_width), axis=1
    ).astype(jnp.bfloat16)
    merged_residual = jnp.mean(
        vision_residual.astype(jnp.float32).reshape(-1, 4, feature_width), axis=1
    )
    partial_value = jnp.dot(
        merged_context,
        lax.all_gather(out_weight, "req", axis=1, tiled=True),
        preferred_element_type=jnp.float32,
    )
    summed = lax.psum(partial_value.astype(jnp.bfloat16), "tp").astype(jnp.float32)
    own_share = lax.dynamic_slice_in_dim(
        summed, lax.axis_index("tp") * feature_width, feature_width, 1
    )
    merged = (merged_residual + layer_scale[None, :] * own_share).astype(jnp.bfloat16)
    merged_count = merged.shape[0]
    counts, starts = request_plan(grid_sizes, image_owner, requests)
    request_ends = starts + counts
    capacity = (IMG_MAX + requests - 1) // requests
    request_ids = jnp.arange(requests, dtype=jnp.int32)
    group_index = jnp.arange(merged_count, dtype=jnp.int32) * requests + device_index
    destination = jnp.sum((request_ends[None, :] <= group_index[:, None]).astype(jnp.int32), axis=1)
    owned_start = jnp.sum(
        jnp.where(destination[:, None] == request_ids[None, :], starts[None, :], 0), axis=1
    )
    target = destination * capacity + (group_index - owned_start) // requests
    usable = destination < requests
    send_slots = jnp.arange(requests * capacity, dtype=jnp.int32)
    placing = ((send_slots[:, None] == target[None, :]) & usable[None, :]).astype(jnp.bfloat16)
    outgoing = jnp.dot(placing, merged, preferred_element_type=jnp.float32).astype(jnp.bfloat16)
    arrived = lax.all_to_all(
        outgoing.reshape(requests, capacity, feature_width),
        "req",
        split_axis=0,
        concat_axis=0,
        tiled=True,
    )
    arrived = arrived.reshape(requests * capacity, feature_width)
    own_request = request_ids == device_index
    own_count = jnp.sum(jnp.where(own_request, counts, 0))
    own_start = jnp.sum(jnp.where(own_request, starts, 0))
    image_from = image_at[0]
    prompt_count = prompt_len[0]
    seq_slots = prompt.shape[1] + IMG_MAX
    slot_index = jnp.arange(seq_slots, dtype=jnp.int32)
    image_row = slot_index - image_from
    in_image = (image_row >= 0) & (image_row < own_count)
    is_live = slot_index < prompt_count + own_count
    from_prompt = is_live & jnp.logical_not(in_image)
    flat_index = (own_start + image_row) % requests * capacity + image_row // requests
    image_pick = ((flat_index[:, None] == send_slots[None, :]) & in_image[:, None]).astype(
        jnp.bfloat16
    )
    prompt_row = jnp.where(slot_index < image_from, slot_index, slot_index - own_count)
    prompt_ids = jnp.arange(prompt.shape[1], dtype=jnp.int32)
    prompt_pick = ((prompt_row[:, None] == prompt_ids[None, :]) & from_prompt[:, None]).astype(
        jnp.bfloat16
    )
    embedded = (
        jnp.dot(image_pick, arrived, preferred_element_type=jnp.float32)
        + jnp.dot(prompt_pick, prompt[0], preferred_element_type=jnp.float32)
    ).astype(jnp.bfloat16)
    gathered = lax.all_gather(embedded, "tp", axis=1, tiled=True)
    normed = normalize(gathered, norm_gain)
    projected = jnp.dot(
        normed,
        lax.all_gather(qkv_weight, "req", axis=0, tiled=True),
        preferred_element_type=jnp.float32,
    )
    cosine_table, sine_table = rope_tables(seq_slots)
    return apply_rope(projected, cosine_table, sine_table).astype(jnp.bfloat16)


def solution(mesh):
    in_specs = (
        P("req", "tp"),
        P("req", "tp"),
        P("tp", "req"),
        P("tp"),
        P("req", None, "tp"),
        P("req"),
        P("req"),
        P(),
        P(),
        P(),
        P("req", "tp"),
    )
    out_specs = P("req", "tp")
    return jax.shard_map(shards, mesh=mesh, in_specs=in_specs, out_specs=out_specs, check_vma=False)
```

profile of v0, /device:TPU:1, one launch (start us, length us, event | category | flops | bytes accessed | tf_op | source)
XLA Modules:
  0.0 352.9 jit_solution(7770393168710454331)
XLA Ops:
  6.5 0.0 copy-start
  6.5 0.0 all-gather.4.cloned.1.call-start
  6.5 0.7 all-gather.4.cloned.1.call-update
  7.3 0.0 all-reduce.2.cloned.1.call-start
  7.3 1.4 reshape.205
  8.7 0.0 copy-start.4
  8.7 0.0 copy-start.1
  8.7 0.6 reduce_sum.78
  9.3 0.8 multiply_bitcast_fusion
  10.1 0.0 copy-start.2
  10.1 91.0 %all-gather.4.cloned.1.call-done = bf16[512,4096]{0,1:T(8,128)(2,1)} async-done(((bf16[512,64]{0,1:T(8,128)(2,1)}), bf16[512,4096]{0,1:T(8,128)(2,1)}) %all-gather.4.cloned.1.call-update) | async-done | bytes 4194320 | tf_op jit(solution)/shard_map/all_gather | solution.py:78
  101.1 4.6 %convolution_convert_fusion = bf16[128,4096]{1,0:T(8,128)(2,1)} fusion(bf16[512,4096]{0,1:T(8,128)(2,1)} %all-gather.4.cloned.1.call-done, f32[128,512]{1,0:T(8,128)S(1)} %reduce_sum.78), kind=kOutput, calls=%fused_computation.5 | convolution fusion | flops 537526272 | bytes 5505024 | tf_op jit(solution)/shard_map/dot_general | solution.py:76
  105.7 0.0 all-reduce.2.cloned.1.call-update
  105.7 0.0 copy-done.4
  105.7 0.1 select_reduce_fusion.1
  105.8 0.1 copy.16
  105.9 0.1 reduce-window.7
  106.0 0.1 reduce
  106.2 0.0 copy-done.1
  106.2 0.3 reshape.203
  106.5 0.0 copy-start.3
  106.5 0.6 reduce_sum.77
  107.2 0.1 convert_reduce_fusion
  107.3 0.7 fusion.38
  108.0 0.1 select_reduce_fusion
  108.1 73.3 %all-reduce.2.cloned.1.call-done = bf16[128,4096]{1,0:T(8,128)(2,1)} async-done(((bf16[128,4096]{1,0:T(8,128)(2,1)}), bf16[128,4096]{1,0:T(8,128)(2,1)}) %all-reduce.2.cloned.1.call-update) | async-done | bytes 1048592 | tf_op jit(solution)/shard_map/psum | solution.py:81
  181.4 0.0 copy-done.2
  181.4 1.1 convolution_convert_fusion.1
  182.5 0.7 reshape.199
  183.3 14.2 %all-to-all-start = ((bf16[64,2,512]{2,1,0:T(2,128)(2,1)}), bf16[64,2,512]{2,1,0:T(2,128)(2,1)S(1)}, u32[]{:S(2)}, u32[]{:S(2)}) async-start(bf16[64,2,512]{2,1,0:T(2,128)(2,1)} %reshape.199), calls=%async_computation | async-start | bytes 262144 | tf_op jit(solution)/shard_map/all_to_all | solution.py:101
  197.4 0.0 all-gather.6.cloned.1.call-start
  199.3 0.6 fusion.37
  199.9 1.3 fusion.30
  201.2 6.6 %all-to-all-done = bf16[64,2,512]{2,1,0:T(2,128)(2,1)S(1)} async-done(((bf16[64,2,512]{2,1,0:T(2,128)(2,1)}), bf16[64,2,512]{2,1,0:T(2,128)(2,1)S(1)}, u32[]{:S(2)}, u32[]{:S(2)}) %all-to-all-start) | async-done | bytes 131104 | tf_op jit(solution)/shard_map/all_to_all | solution.py:101
  207.8 0.1 reshape.200
  207.9 0.3 fusion.14
  208.2 0.0 copy-done
  208.2 1.1 fusion.7
  209.3 0.0 all-gather.6.cloned.1.call-update
  209.3 0.0 all-gather.8.cloned.1.call-start
  209.3 0.5 all-gather.8.cloned.1.call-update
  209.9 0.4 fusion.21
  210.3 40.0 %all-gather.6.cloned.1.call-done = bf16[384,4096]{1,0:T(8,128)(2,1)} async-done(((bf16[384,512]{1,0:T(8,128)(2,1)}), bf16[384,4096]{1,0:T(8,128)(2,1)}) %all-gather.6.cloned.1.call-update) | async-done | bytes 3145744 | tf_op jit(solution)/shard_map/all_gather | solution.py:133
  250.3 2.6 fusion
  252.9 85.4 %all-gather.8.cloned.1.call-done = bf16[4096,768]{1,0:T(8,128)(2,1)} async-done(((bf16[64,768]{1,0:T(8,128)(2,1)}), bf16[4096,768]{1,0:T(8,128)(2,1)}) %all-gather.8.cloned.1.call-update) | async-done | bytes 6291472 | tf_op jit(solution)/shard_map/all_gather | solution.py:137
  338.3 0.0 copy-done.3
  338.3 6.7 %fusion.3 = f32[384,768]{0,1:T(8,128)S(1)} fusion(bf16[4096,768]{1,0:T(8,128)(2,1)} %all-gather.8.cloned.1.call-done, bf16[384,4096]{1,0:T(8,128)(2,1)} %all-gather.6.cloned.1.call-done, f32[4096]{0:T(1024)S(1)} %copy-done.3, f32[384]{0:T(512)S(1)} %add_rsqrt_fusion), kind=kOutput, calls=%fused_computation.6 | convolution fusion | flops 2422210560 | bytes 10634752 | tf_op jit(solution)/shard_map/dot_general | solution.py:135
  345.0 0.1 subtract_convert_fusion
  345.2 0.1 pad_maximum_fusion
  345.2 1.1 copy.18
  (6 shorter events, 0.1 us)
Async XLA Ops:
  6.5 201.7 %copy-start = (bf16[1,256,512]{2,1,0:T(8,128)(2,1)S(1)}, bf16[1,256,512]{2,1,0:T(8,128)(2,1)}, u32[]{:S(2)}) copy-start(bf16[1,256,512]{2,1,0:T(8,128)(2,1)} %param.15) | copy-start | bytes 786436
  6.5 94.5 %all-gather.4.cloned.1.call-start = ((), (), s32[]{:S(2)}) async-start(), calls=%async_computation.1 | async-start | bytes 4259840 | tf_op jit(solution)/shard_map/all_gather | solution.py:78
  7.3 174.2 %all-reduce.2.cloned.1.call-start = ((), (), s32[]{:S(2)}) async-start(), calls=%async_computation.2 | async-start | bytes 2097152 | tf_op jit(solution)/shard_map/psum | solution.py:81
  8.7 97.0 %copy-start.4 = (s32[128]{0:T(128)S(1)}, s32[128]{0:T(128)}, u32[]{:S(2)}) copy-start(s32[128]{0:T(128)} %param.19) | copy-start | bytes 1540
  8.7 97.5 %copy-start.1 = (bf16[512,512]{1,0:T(8,128)(2,1)S(1)}, bf16[512,512]{1,0:T(8,128)(2,1)}, u32[]{:S(2)}) copy-start(bf16[512,512]{1,0:T(8,128)(2,1)} %param.12) | copy-start | bytes 1572868
  10.1 171.3 %copy-start.2 = (f32[512]{0:T(512)S(1)}, f32[512]{0:T(512)}, u32[]{:S(2)}) copy-start(f32[512]{0:T(512)} %param.14) | copy-start | bytes 6148
  106.5 231.8 %copy-start.3 = (f32[4096]{0:T(1024)S(1)}, f32[4096]{0:T(1024)}, u32[]{:S(2)}) copy-start(f32[4096]{0:T(1024)} %param.20) | copy-start | bytes 49156
  183.3 24.5 %all-to-all-start = ((bf16[64,2,512]{2,1,0:T(2,128)(2,1)}), bf16[64,2,512]{2,1,0:T(2,128)(2,1)S(1)}, u32[]{:S(2)}, u32[]{:S(2)}) async-start(bf16[64,2,512]{2,1,0:T(2,128)(2,1)} %reshape.199), calls=%async_computation | async-start | bytes 262144 | tf_op jit(solution)/shard_map/all_to_all | solution.py:101
  197.4 52.9 %all-gather.6.cloned.1.call-start = ((), (), s32[]{:S(2)}) async-start(), calls=%async_computation.3 | async-start | bytes 3538944 | tf_op jit(solution)/shard_map/all_gather | solution.py:133
  209.3 129.0 %all-gather.8.cloned.1.call-start = ((), (), s32[]{:S(2)}) async-start(), calls=%async_computation.4 | async-start | bytes 6389760 | tf_op jit(solution)/shard_map/all_gather | solution.py:137
Sparse Core Ops, SparseCore 0:
  10.7 90.2 all-gather.3
  105.8 75.5 all-reduce.1
  209.4 40.8 all-gather.5
  253.5 84.7 all-gather.7
where the time goes:
time: 353 us
  waiting for transfers between devices  298 us (84%)
  between operations  15.2 us (4%)
  starting transfers between devices  14.3 us (4%)
  matrix products  13.8 us (4%)
  other arithmetic  8.27 us (2%)
  local copies, waits for them, and re-layouts  3.69 us (1%)
    all_gather x1, waiting for transfers between devices, shards(): lax.all_gather(out_weight, 'req', axis=1, tiled=True)  91 us
    all_gather x1, waiting for transfers between devices, shards(): lax.all_gather(qkv_weight, 'req', axis=0, tiled=True)  85.4 us
    psum x1, waiting for transfers between devices, shards(): lax.psum(partial_value.astype(jnp.bfloat16), 'tp').astype(jnp.float32)  73.3 us
    all_gather x1, waiting for transfers between devices, shards(): gathered = lax.all_gather(embedded, 'tp', axis=1, tiled=True)  40 us
    all_to_all x1, starting transfers between devices, shards(): lax.all_to_all(outgoing.reshape(requests, capacity, feature_width), 'req'...  14.2 us
  transfers between devices with their start and end apart: 5, of which 5 were waited for; matrix products, arithmetic and copies ran while one was open for 3% of the time, Pallas kernels for 0%

commit v1 on v0

--- a/solution.py
+++ b/solution.py
@@ -2,6 +2,7 @@
 import jax.numpy as jnp
 from jax import lax
 from jax.sharding import PartitionSpec as P
+from jax.lax import axis_index, ppermute, psum
 
 HEAD = 128
 GROUP = 4
@@ -130,7 +131,14 @@
         jnp.dot(image_pick, arrived, preferred_element_type=jnp.float32)
         + jnp.dot(prompt_pick, prompt[0], preferred_element_type=jnp.float32)
     ).astype(jnp.bfloat16)
-    gathered = lax.all_gather(embedded, "tp", axis=1, tiled=True)
+    full_n = psum(1, axis_name="tp")
+    log = [embedded]
+    for k in tuple(range(full_n - 1)):
+        met_up = ppermute(log[-1], "tp", [(j, (j + 1) % full_n) for j in range(full_n)])
+        log.append(met_up)
+    a_now = jnp.concatenate(log[::-1], axis=1)
+    lower = axis_index("tp")
+    gathered = jnp.roll(a_now, (lower + 1) * embedded.shape[1], axis=1)
     normed = normalize(gathered, norm_gain)
     projected = jnp.dot(
         normed,

time: 353 us -> 311 us (0.88); the launches traced: 353 us -> 306 us
  waiting for transfers between devices: 298 us -> 235 us
  starting transfers between devices: 14.3 us -> 28.4 us
    all_gather x1, waiting for transfers between devices: 85.4 us -> 0.02 us  [shards(): lax.all_gather(qkv_weight, 'req', axis=0, tiled=True)]
    ppermute x0 -> x7, waiting for transfers between devices: none -> 63 us  [shards(): ppermute(log[-1], 'tp', [(j, (j + 1) % full_n) for j in range(full_n)])]
    all_gather x1 -> x0, waiting for transfers between devices: 40 us -> none  [shards(): gathered = lax.all_gather(embedded, 'tp', axis=1, tiled=True)]
    ppermute x0 -> x7, starting transfers between devices: none -> 14.1 us  [shards(): ppermute(log[-1], 'tp', [(j, (j + 1) % full_n) for j in range(full_n)])]
  transfers between devices with their start and end apart: 5 -> 11, of which waited for: 5 -> 10; matrix products, arithmetic and copies ran while one was open for 3% -> 4% of each run, Pallas kernels for 0% -> 0%
where the time goes in v1:
time: 311 us; the launch traced here: 306 us
  waiting for transfers between devices  235 us (76%)
  starting transfers between devices  28.4 us (9%)
  between operations  15.5 us (5%)
  matrix products  13.2 us (4%)
  local copies, waits for them, and re-layouts  6.99 us (2%)
  other arithmetic  6.23 us (2%)
    all_gather x1, waiting for transfers between devices, shards(): lax.all_gather(out_weight, 'req', axis=1, tiled=True)  91.7 us
    psum x1, waiting for transfers between devices, shards(): lax.psum(partial_value.astype(jnp.bfloat16), 'tp').astype(jnp.float32)  72.7 us
    ppermute x7, waiting for transfers between devices, shards(): ppermute(log[-1], 'tp', [(j, (j + 1) % full_n) for j in range(full_n)])  63 us
    all_to_all x1, starting transfers between devices, shards(): lax.all_to_all(outgoing.reshape(requests, capacity, feature_width), 'req'...  14.2 us
    ppermute x7, starting transfers between devices, shards(): ppermute(log[-1], 'tp', [(j, (j + 1) % full_n) for j in range(full_n)])  14.1 us
    dot_general x1, matrix products, shards(): jnp.dot(normed, lax.all_gather(qkv_weight, 'req', axis=0, tiled=True), pr...  6.75 us
    all_to_all x1, waiting for transfers between devices, shards(): lax.all_to_all(outgoing.reshape(requests, capacity, feature_width), 'req'...  6.59 us
  transfers between devices with their start and end apart: 11, of which 10 were waited for; matrix products, arithmetic and copies ran while one was open for 4% of the time, Pallas kernels for 0%

profile of v1, /device:TPU:1, one launch (start us, length us, event | category | flops | bytes accessed | tf_op | source)
XLA Modules:
  0.0 305.6 jit_solution(2628359597963781023)
XLA Ops:
  6.5 0.0 copy-start
  6.5 0.0 copy-start.6
  6.5 0.0 copy-start.7
  6.5 0.0 all-gather.3.cloned.1.call-start
  6.6 0.7 all-gather.3.cloned.1.call-update
  7.3 0.0 copy-start.4
  7.3 0.0 all-reduce.2.cloned.1.call-start
  7.3 1.4 reshape.205
  8.7 0.6 reduce_sum.78
  9.3 91.7 %all-gather.3.cloned.1.call-done = bf16[512,4096]{0,1:T(8,128)(2,1)} async-done(((bf16[512,64]{0,1:T(8,128)(2,1)}), bf16[512,4096]{0,1:T(8,128)(2,1)}) %all-gather.3.cloned.1.call-update) | async-done | bytes 4194320 | tf_op jit(solution)/shard_map/all_gather | solution.py:79
  101.1 4.7 %convolution_convert_fusion = bf16[128,4096]{1,0:T(8,128)(2,1)} fusion(bf16[512,4096]{0,1:T(8,128)(2,1)} %all-gather.3.cloned.1.call-done, f32[128,512]{1,0:T(8,128)S(1)} %reduce_sum.78), kind=kOutput, calls=%fused_computation.5 | convolution fusion | flops 537526272 | bytes 5505024 | tf_op jit(solution)/shard_map/dot_general | solution.py:77
  105.7 0.0 all-reduce.2.cloned.1.call-update
  105.8 0.0 all-gather.5.cloned.1.call-start
  105.8 0.7 all-gather.5.cloned.1.call-update
  106.5 0.0 copy-done.6
  106.5 0.0 copy-done.7
  106.5 0.1 select_reduce_fusion.1
  106.6 0.1 copy.16
  106.7 0.1 reduce-window.7
  106.8 0.1 reduce
  107.0 0.0 copy-done.2
  107.0 0.3 reshape.203
  107.3 0.6 reduce_sum.77
  107.9 0.1 convert_reduce_fusion
  108.0 0.7 fusion.39
  108.7 0.1 select_reduce_fusion
  108.8 72.7 %all-reduce.2.cloned.1.call-done = bf16[128,4096]{1,0:T(8,128)(2,1)} async-done(((bf16[128,4096]{1,0:T(8,128)(2,1)}), bf16[128,4096]{1,0:T(8,128)(2,1)}) %all-reduce.2.cloned.1.call-update) | async-done | bytes 1048592 | tf_op jit(solution)/shard_map/psum | solution.py:82
  181.5 0.0 copy-done.4
  181.5 1.1 convolution_convert_fusion.1
  182.6 0.7 reshape.199
  183.3 14.2 %all-to-all-start = ((bf16[64,2,512]{2,1,0:T(2,128)(2,1)}), bf16[64,2,512]{2,1,0:T(2,128)(2,1)S(1)}, u32[]{:S(2)}, u32[]{:S(2)}) async-start(bf16[64,2,512]{2,1,0:T(2,128)(2,1)} %reshape.199), calls=%async_computation | async-start | bytes 262144 | tf_op jit(solution)/shard_map/all_to_all | solution.py:102
  199.4 0.6 fusion.38
  200.0 1.2 fusion.31
  201.3 6.6 %all-to-all-done = bf16[64,2,512]{2,1,0:T(2,128)(2,1)S(1)} async-done(((bf16[64,2,512]{2,1,0:T(2,128)(2,1)}), bf16[64,2,512]{2,1,0:T(2,128)(2,1)S(1)}, u32[]{:S(2)}, u32[]{:S(2)}) %all-to-all-start) | async-done | bytes 131104 | tf_op jit(solution)/shard_map/all_to_all | solution.py:102
  207.9 0.1 reshape.200
  207.9 0.3 fusion.15
  208.2 0.0 copy-done
  208.2 0.3 fusion.8
  208.6 2.7 collective-permute-start
  211.3 10.8 %collective-permute-done = bf16[384,512]{1,0:T(8,128)(2,1)S(1)} collective-permute-done((bf16[384,512]{1,0:T(8,128)(2,1)S(1)}, bf16[384,512]{1,0:T(8,128)(2,1)S(1)}, u32[]{:S(2)}, u32[]{:S(2)}) %collective-permute-start) | collective-permute-done | bytes 393248 | tf_op jit(solution)/shard_map/ppermute | solution.py:137
  222.1 1.9 collective-permute-start.1
  224.0 10.7 %collective-permute-done.1 = bf16[384,512]{1,0:T(8,128)(2,1)S(1)} collective-permute-done((bf16[384,512]{1,0:T(8,128)(2,1)S(1)}, bf16[384,512]{1,0:T(8,128)(2,1)S(1)}, u32[]{:S(2)}, u32[]{:S(2)}) %collective-permute-start.1) | collective-permute-done | bytes 393248 | tf_op jit(solution)/shard_map/ppermute | solution.py:137
  234.7 1.9 collective-permute-start.2
  236.6 9.8 %collective-permute-done.2 = bf16[384,512]{1,0:T(8,128)(2,1)S(1)} collective-permute-done((bf16[384,512]{1,0:T(8,128)(2,1)S(1)}, bf16[384,512]{1,0:T(8,128)(2,1)S(1)}, u32[]{:S(2)}, u32[]{:S(2)}) %collective-permute-start.2) | collective-permute-done | bytes 393248 | tf_op jit(solution)/shard_map/ppermute | solution.py:137
  246.4 1.9 collective-permute-start.3
  248.3 9.0 %collective-permute-done.3 = bf16[384,512]{1,0:T(8,128)(2,1)S(1)} collective-permute-done((bf16[384,512]{1,0:T(8,128)(2,1)S(1)}, bf16[384,512]{1,0:T(8,128)(2,1)S(1)}, u32[]{:S(2)}, u32[]{:S(2)}) %collective-permute-start.3) | collective-permute-done | bytes 393248 | tf_op jit(solution)/shard_map/ppermute | solution.py:137
  257.4 1.9 collective-permute-start.4
  259.3 8.1 %collective-permute-done.4 = bf16[384,512]{1,0:T(8,128)(2,1)S(1)} collective-permute-done((bf16[384,512]{1,0:T(8,128)(2,1)S(1)}, bf16[384,512]{1,0:T(8,128)(2,1)S(1)}, u32[]{:S(2)}, u32[]{:S(2)}) %collective-permute-start.4) | collective-permute-done | bytes 393248 | tf_op jit(solution)/shard_map/ppermute | solution.py:137
  267.4 1.9 collective-permute-start.5
  269.3 7.8 %collective-permute-done.5 = bf16[384,512]{1,0:T(8,128)(2,1)S(1)} collective-permute-done((bf16[384,512]{1,0:T(8,128)(2,1)S(1)}, bf16[384,512]{1,0:T(8,128)(2,1)S(1)}, u32[]{:S(2)}, u32[]{:S(2)}) %collective-permute-start.5) | collective-permute-done | bytes 393248 | tf_op jit(solution)/shard_map/ppermute | solution.py:137
  277.1 1.9 collective-permute-start.6
  279.1 1.1 fusion.22
  280.1 6.7 %collective-permute-done.6 = bf16[384,512]{1,0:T(8,128)(2,1)S(1)} collective-permute-done((bf16[384,512]{1,0:T(8,128)(2,1)S(1)}, bf16[384,512]{1,0:T(8,128)(2,1)S(1)}, u32[]{:S(2)}, u32[]{:S(2)}) %collective-permute-start.6) | collective-permute-done | bytes 393248 | tf_op jit(solution)/shard_map/ppermute | solution.py:137
  287.0 0.0 copy-start.5
  287.6 0.0 copy-start.1
  287.6 2.7 copy-done.1
  290.3 0.7 fusion
  291.0 0.0 all-gather.5.cloned.1.call-done
  291.0 0.0 copy-done.5
  291.0 6.7 %fusion.3 = f32[384,768]{0,1:T(8,128)S(1)} fusion(bf16[4096,768]{1,0:T(8,128)(2,1)} %all-gather.5.cloned.1.call-done, f32[4096]{0:T(1024)S(1)} %copy-done.5, f32[384]{0:T(512)S(1)} %add_rsqrt_fusion, bf16[384,8192]{1,0:T(8,128)(2,1)} %copy-done.1, s32[]{:T(128)S(6)} %select_n.71), kind=kOutput, calls=%fused_computation.6 | convolution fusion | flops 2422210560 | bytes 10634756 | tf_op jit(solution)/shard_map/dot_general | solution.py:143
  297.8 0.0 copy-done.3
  297.8 0.1 subtract_convert_fusion
  297.9 0.1 pad_maximum_fusion
  298.0 1.1 copy.18
  (25 shorter events, 0.7 us)
Async XLA Ops:
  6.5 201.7 %copy-start = (bf16[1,256,512]{2,1,0:T(8,128)(2,1)S(1)}, bf16[1,256,512]{2,1,0:T(8,128)(2,1)}, u32[]{:S(2)}) copy-start(bf16[1,256,512]{2,1,0:T(8,128)(2,1)} %param.15) | copy-start | bytes 786436
  6.5 100.0 %copy-start.6 = (s32[128,2]{0,1:T(2,128)S(1)}, s32[128,2]{0,1:T(2,128)}, u32[]{:S(2)}) copy-start(s32[128,2]{0,1:T(2,128)} %param.18) | copy-start | bytes 3076
  6.5 100.0 %copy-start.7 = (s32[128]{0:T(128)S(1)}, s32[128]{0:T(128)}, u32[]{:S(2)}) copy-start(s32[128]{0:T(128)} %param.19) | copy-start | bytes 1540
  6.5 100.4 %copy-start.2 = (bf16[512,512]{1,0:T(8,128)(2,1)S(1)}, bf16[512,512]{1,0:T(8,128)(2,1)}, u32[]{:S(2)}) copy-start(bf16[512,512]{1,0:T(8,128)(2,1)} %param.12) | copy-start | bytes 1572868
  6.5 94.5 %all-gather.3.cloned.1.call-start = ((), (), s32[]{:S(2)}) async-start(), calls=%async_computation.1 | async-start | bytes 4259840 | tf_op jit(solution)/shard_map/all_gather | solution.py:79
  7.3 174.2 %copy-start.4 = (f32[512]{0:T(512)S(1)}, f32[512]{0:T(512)}, u32[]{:S(2)}) copy-start(f32[512]{0:T(512)} %param.14) | copy-start | bytes 6148
  7.3 174.2 %all-reduce.2.cloned.1.call-start = ((), (), s32[]{:S(2)}) async-start(), calls=%async_computation.2 | async-start | bytes 2097152 | tf_op jit(solution)/shard_map/psum | solution.py:82
  105.8 185.2 %all-gather.5.cloned.1.call-start = ((), (), s32[]{:S(2)}) async-start(), calls=%async_computation.3 | async-start | bytes 6389760 | tf_op jit(solution)/shard_map/all_gather | solution.py:145
  183.3 24.5 %all-to-all-start = ((bf16[64,2,512]{2,1,0:T(2,128)(2,1)}), bf16[64,2,512]{2,1,0:T(2,128)(2,1)S(1)}, u32[]{:S(2)}, u32[]{:S(2)}) async-start(bf16[64,2,512]{2,1,0:T(2,128)(2,1)} %reshape.199), calls=%async_computation | async-start | bytes 262144 | tf_op jit(solution)/shard_map/all_to_all | solution.py:102
  208.6 13.5 %collective-permute-start = (bf16[384,512]{1,0:T(8,128)(2,1)S(1)}, bf16[384,512]{1,0:T(8,128)(2,1)S(1)}, u32[]{:S(2)}, u32[]{:S(2)}) collective-permute-start(bf16[384,512]{1,0:T(8,128)(2,1)S(1)} %fusion.8), channel_id=1, source_target_pairs={{0,1},{1,2},{2,3},{3,4},{4,5},{5,6},{6,7},{7,0},{8,9},{9,10},{10,1... | collective-permute-start | bytes 1179656 | tf_op jit(solution)/shard_map/ppermute | solution.py:137
  222.1 12.6 %collective-permute-start.1 = (bf16[384,512]{1,0:T(8,128)(2,1)S(1)}, bf16[384,512]{1,0:T(8,128)(2,1)S(1)}, u32[]{:S(2)}, u32[]{:S(2)}) collective-permute-start(bf16[384,512]{1,0:T(8,128)(2,1)S(1)} %collective-permute-done), channel_id=1, source_target_pairs={{0,1},{1,2},{2,3},{3,4},{4,5},{5,6},{6,7},{7,0},{8,9},{9,10},{10,1... | collective-permute-start | bytes 1179656 | tf_op jit(solution)/shard_map/ppermute | solution.py:137
  234.7 11.8 %collective-permute-start.2 = (bf16[384,512]{1,0:T(8,128)(2,1)S(1)}, bf16[384,512]{1,0:T(8,128)(2,1)S(1)}, u32[]{:S(2)}, u32[]{:S(2)}) collective-permute-start(bf16[384,512]{1,0:T(8,128)(2,1)S(1)} %collective-permute-done.1), channel_id=1, source_target_pairs={{0,1},{1,2},{2,3},{3,4},{4,5},{5,6},{6,7},{7,0},{8,9},{9,10},{10,1... | collective-permute-start | bytes 1179656 | tf_op jit(solution)/shard_map/ppermute | solution.py:137
  246.4 10.9 %collective-permute-start.3 = (bf16[384,512]{1,0:T(8,128)(2,1)S(1)}, bf16[384,512]{1,0:T(8,128)(2,1)S(1)}, u32[]{:S(2)}, u32[]{:S(2)}) collective-permute-start(bf16[384,512]{1,0:T(8,128)(2,1)S(1)} %collective-permute-done.2), channel_id=1, source_target_pairs={{0,1},{1,2},{2,3},{3,4},{4,5},{5,6},{6,7},{7,0},{8,9},{9,10},{10,1... | collective-permute-start | bytes 1179656 | tf_op jit(solution)/shard_map/ppermute | solution.py:137
  257.4 10.0 %collective-permute-start.4 = (bf16[384,512]{1,0:T(8,128)(2,1)S(1)}, bf16[384,512]{1,0:T(8,128)(2,1)S(1)}, u32[]{:S(2)}, u32[]{:S(2)}) collective-permute-start(bf16[384,512]{1,0:T(8,128)(2,1)S(1)} %collective-permute-done.3), channel_id=1, source_target_pairs={{0,1},{1,2},{2,3},{3,4},{4,5},{5,6},{6,7},{7,0},{8,9},{9,10},{10,1... | collective-permute-start | bytes 1179656 | tf_op jit(solution)/shard_map/ppermute | solution.py:137
  267.4 9.7 %collective-permute-start.5 = (bf16[384,512]{1,0:T(8,128)(2,1)S(1)}, bf16[384,512]{1,0:T(8,128)(2,1)S(1)}, u32[]{:S(2)}, u32[]{:S(2)}) collective-permute-start(bf16[384,512]{1,0:T(8,128)(2,1)S(1)} %collective-permute-done.4), channel_id=1, source_target_pairs={{0,1},{1,2},{2,3},{3,4},{4,5},{5,6},{6,7},{7,0},{8,9},{9,10},{10,1... | collective-permute-start | bytes 1179656 | tf_op jit(solution)/shard_map/ppermute | solution.py:137
  277.1 9.7 %collective-permute-start.6 = (bf16[384,512]{1,0:T(8,128)(2,1)S(1)}, bf16[384,512]{1,0:T(8,128)(2,1)S(1)}, u32[]{:S(2)}, u32[]{:S(2)}) collective-permute-start(bf16[384,512]{1,0:T(8,128)(2,1)S(1)} %collective-permute-done.5), channel_id=1, source_target_pairs={{0,1},{1,2},{2,3},{3,4},{4,5},{5,6},{6,7},{7,0},{8,9},{9,10},{10,1... | collective-permute-start | bytes 1179656 | tf_op jit(solution)/shard_map/ppermute | solution.py:137
  287.0 4.0 %copy-start.5 = (f32[4096]{0:T(1024)S(1)}, f32[4096]{0:T(1024)}, u32[]{:S(2)}) copy-start(f32[4096]{0:T(1024)} %param.20) | copy-start | bytes 49156
  287.6 2.7 copy-start.1
  291.0 6.8 %copy-start.3 = (f32[384,64]{0,1:T(8,128)S(1)}, f32[384,64]{0,1:T(8,128)}, u32[]{:S(2)}) copy-start(f32[384,64]{0,1:T(8,128)} %get-tuple-element.12) | copy-start | bytes 294916
Sparse Core Ops, SparseCore 0:
  10.7 90.2 all-gather.2
  105.9 75.5 all-reduce.1
  184.8 88.4 all-gather.4
